TPU v7x, 128 devices: a whole 4x4x4 slice. The times are simulated.
128 devices in a mesh: leaf: 16 (over y, z), ctx: 8 (over x, core).
Axes of the slice: x: 4, y: 4, z: 4, core: 2. Of those that a mesh axis runs over, the one named last changes fastest.
Arguments:
- query_key_value_rows: bfloat16 [16384, 7168], P(('leaf', 'ctx')), may hold values from -6 to 6
- cotangent: bfloat16 [16384, 5120], P(('leaf', 'ctx')), may hold values from -6 to 6
- out_weight: bfloat16 [5120, 5120], P('ctx'), may hold values from -0.078125 to 0.078125
- parents: int32 [16, 8], P('leaf'), may hold values from 0 to 6, as said below
- rollout_spans: int32 [16384], P('leaf'), may hold values from 64 to 4096
Outputs:
- qkv_grad: bfloat16 [16384, 7168], P(('leaf', 'ctx'))
- weight_grad: bfloat16 [5120, 5120], P('ctx')
Inputs may be any that keep to these rules, and one draw needn't show every extreme that they name: parents[t, 0] = 0, every later block's parent is an earlier block of the same tree, and the last block's parent is the block just before it.
All inputs are finite; a program needn't handle non-finite values.
Results may differ from a plain program's by a relative error of at most 0.012.
The roundings to bfloat16 on the way count: a program that leaves them out, or rounds other values in their place, can miss the bound.
Values may be sent and summed in bfloat16 or wider, within the bound.
No kernel may reach another device: no remote copies, remote signals or barrier semaphores. Data moves between devices by JAX's collectives and lax.ppermute only.
A program may use at most 192 MiB of HBM per device.

v0:
```python
import math

import jax
import jax.numpy as jnp
from jax import lax
from jax.sharding import PartitionSpec as P

QUERY_HEADS = 40
KEY_VALUE_HEADS = 8
HEAD_SIZE = 128
BLK = 128


log_base = 1024.0


def ancestors(parents):
    number = parents.shape[0]
    indices = jnp.arange(number, dtype=jnp.int32)

    def advance(iteration, state):
        current, reached = state
        current = jnp.sum(
            jnp.where(current[:, None] == indices[None, :], parents[None, :], 0), axis=1
        )
        return (current, reached | (current[:, None] == indices[None, :]))

    return lax.fori_loop(0, number, advance, (indices, indices[:, None] == indices[None, :]))[1]


def token_mask(reached, first_row, query_count, key_count):
    query_pos = first_row + jnp.arange(query_count, dtype=jnp.int32)
    key_pos = jnp.arange(key_count, dtype=jnp.int32)
    block_part = reached[first_row // BLK : (first_row + query_count) // BLK, : key_count // BLK]
    expanded = jnp.repeat(jnp.repeat(block_part, BLK, axis=0), BLK, axis=1)
    same_block = (query_pos // BLK)[:, None] == (key_pos // BLK)[None, :]
    return expanded & (jnp.logical_not(same_block) | (key_pos[None, :] <= query_pos[:, None]))


def span_softness(rollout_spans):
    return jnp.log(rollout_spans.astype(jnp.float32)) * (
        1.0 / (math.log(log_base) * math.sqrt(HEAD_SIZE))
    )


def contract_rows(left, right):
    return lax.dot_general(
        left, right, (((0,), (0,)), ((), ())), preferred_element_type=jnp.float32
    )


def contract_cols(left, right):
    return lax.dot_general(
        left, right, (((1,), (1,)), ((), ())), preferred_element_type=jnp.float32
    )


def local(query_key_value_rows, cotangent, out_weight, parents, rollout_spans):
    queries_per_group = QUERY_HEADS // KEY_VALUE_HEADS
    head_rows = lax.all_to_all(query_key_value_rows, "ctx", split_axis=1, concat_axis=0, tiled=True)
    tree_len = head_rows.shape[0]
    kv_local = head_rows.shape[1] // ((queries_per_group + 2) * HEAD_SIZE)
    heads_local = kv_local * queries_per_group
    grouped = head_rows.reshape(tree_len, kv_local, queries_per_group + 2, HEAD_SIZE)
    asking_matrix = grouped[:, :, :queries_per_group]
    lookup_matrix = grouped[:, :, queries_per_group]
    value_rows = grouped[:, :, queries_per_group + 1]
    softness_multiplier = span_softness(rollout_spans)
    reached = ancestors(parents[0])
    block_len = min(512, tree_len)
    block_total = tree_len // block_len
    masks = []
    total_parts = []
    attended_parts = []
    for block_id in range(block_total):
        opening_slot = block_id * block_len
        closing_slot = opening_slot + block_len
        allowed = token_mask(reached, opening_slot, block_len, closing_slot)
        masks.append(allowed)
        attention_logits = jnp.einsum(
            "zpyr,kpr->pyzk",
            asking_matrix[opening_slot:closing_slot],
            lookup_matrix[:closing_slot],
            preferred_element_type=jnp.float32,
        )
        attention_logits = jnp.where(
            allowed[None, None],
            attention_logits * softness_multiplier[opening_slot:closing_slot][None, None, :, None],
            -jnp.inf,
        )
        peak_score = jnp.max(attention_logits, axis=-1, keepdims=True)
        log_total = peak_score + jnp.log(
            jnp.sum(jnp.exp(attention_logits - peak_score), axis=-1, keepdims=True)
        )
        weights_low = jnp.exp(attention_logits - log_total).astype(jnp.bfloat16)
        attended_parts.append(
            jnp.einsum(
                "gjts,sgd->tgjd",
                weights_low,
                value_rows[:closing_slot],
                preferred_element_type=jnp.float32,
            ).astype(jnp.bfloat16)
        )
        total_parts.append(log_total[..., 0])
    attended = jnp.concatenate(attended_parts, axis=0)
    log_totals = jnp.concatenate(total_parts, axis=2)
    flat_out = attended.reshape(tree_len, heads_local * HEAD_SIZE)
    shard_rows = lax.all_gather(cotangent, "ctx", axis=0, tiled=True)
    weight_acc = contract_rows(flat_out, shard_rows)
    local_grad = contract_cols(shard_rows, out_weight).astype(jnp.bfloat16)
    weight_acc, output_gradient = (weight_acc, local_grad)
    weight_total = lax.psum(weight_acc, "leaf").astype(jnp.bfloat16)
    key_acc = jnp.zeros((tree_len, kv_local, HEAD_SIZE), jnp.float32)
    value_acc = jnp.zeros((tree_len, kv_local, HEAD_SIZE), jnp.float32)
    query_parts = []
    for head_id in range(heads_local):
        kv_id = head_id // queries_per_group
        inner = head_id % queries_per_group
        query_blocks = []
        for block_id in range(block_total):
            opening_slot = block_id * block_len
            closing_slot = opening_slot + block_len
            query_now = asking_matrix[opening_slot:closing_slot, kv_id, inner]
            keys_now = lookup_matrix[:closing_slot, kv_id]
            values_now = value_rows[:closing_slot, kv_id]
            line_multiplier = softness_multiplier[opening_slot:closing_slot][:, None]
            attention_logits = jnp.where(
                masks[block_id], contract_cols(query_now, keys_now) * line_multiplier, -jnp.inf
            )
            attention_probabilities = jnp.exp(
                attention_logits - log_totals[kv_id, inner, opening_slot:closing_slot][:, None]
            )
            grad_rows = output_gradient[
                opening_slot:closing_slot, head_id * HEAD_SIZE : (head_id + 1) * HEAD_SIZE
            ]
            own_rows = attended[opening_slot:closing_slot, kv_id, inner]
            probability_cotangent = contract_cols(grad_rows, values_now)
            middle_point = jnp.sum(
                grad_rows.astype(jnp.float32) * own_rows.astype(jnp.float32), axis=1
            )
            logit_cotangent = (
                attention_probabilities
                * (probability_cotangent - middle_point[:, None])
                * line_multiplier
            ).astype(jnp.bfloat16)
            query_blocks.append(
                jnp.dot(logit_cotangent, keys_now, preferred_element_type=jnp.float32).astype(
                    jnp.bfloat16
                )
            )
            key_acc = key_acc.at[:closing_slot, kv_id].add(
                contract_rows(logit_cotangent, query_now)
            )
            value_acc = value_acc.at[:closing_slot, kv_id].add(
                contract_rows(attention_probabilities.astype(jnp.bfloat16), grad_rows)
            )
        query_parts.append(jnp.concatenate(query_blocks, axis=0))
    query_grad = jnp.stack(query_parts, axis=1).reshape(
        tree_len, kv_local, queries_per_group, HEAD_SIZE
    )
    gradients = jnp.concatenate(
        [
            query_grad,
            key_acc.astype(jnp.bfloat16)[:, :, None],
            value_acc.astype(jnp.bfloat16)[:, :, None],
        ],
        axis=2,
    )
    gradients = gradients.reshape(tree_len, kv_local * (queries_per_group + 2) * HEAD_SIZE)
    returned = lax.all_to_all(gradients, "ctx", split_axis=0, concat_axis=1, tiled=True)
    return (returned, weight_total)


def solution(mesh):
    placed = (
        P(("leaf", "ctx"), None),
        P(("leaf", "ctx"), None),
        P("ctx", None),
        P("leaf", None),
        P("leaf"),
    )
    return jax.shard_map(
        local,
        mesh=mesh,
        in_specs=placed,
        out_specs=(P(("leaf", "ctx"), None), P("ctx", None)),
        check_vma=False,
    )
```

profile of v0, /device:TPU:1, one launch (start us, length us, event | category | flops | bytes accessed | tf_op | source)
XLA Modules:
  0.0 449.3 jit_solution(9614831033946304401)
XLA Ops:
  7.2 0.7 all-gather.2.cloned.1.call-update
  7.9 3.9 copy.35
  11.8 5.9 %all-to-all-start = ((bf16[128,8,896]{0,2,1:T(8,128)(2,1)}), bf16[128,8,896]{0,2,1:T(8,128)(2,1)S(1)}, u32[]{:S(2)}, u32[]{:S(2)}) async-start(bf16[128,8,896]{0,2,1:T(8,128)(2,1)} %bitcast.482), calls=%async_computation | async-start | bytes 3670016 | tf_op jit(solution)/shard_map/all_to_all | solution.py:60
  17.7 2.2 while.34
  20.0 1.6 broadcast_in_dim.71
  22.0 0.4 copy.38
  22.4 1.6 broadcast_in_dim.76
  24.0 0.8 fusion.14
  24.9 1.0 copy.42
  25.9 28.5 %all-to-all-done = bf16[128,8,896]{0,2,1:T(8,128)(2,1)S(1)} async-done(((bf16[128,8,896]{0,2,1:T(8,128)(2,1)}), bf16[128,8,896]{0,2,1:T(8,128)(2,1)S(1)}, u32[]{:S(2)}, u32[]{:S(2)}) %all-to-all-start) | async-done | bytes 1835040 | tf_op jit(solution)/shard_map/all_to_all | solution.py:60
  54.4 2.4 copy.36
  56.8 3.0 reshape.966
  59.8 1.0 fusion.8
  60.9 1.1 exponential_reduce_fusion.1
  62.0 1.8 fusion.3
  63.8 2.2 exponential_reduce_fusion
  66.0 1.6 fusion.54
  67.6 3.6 fusion.51
  71.2 1.3 pad_maximum_fusion.1
  72.5 1.4 fusion.37
  74.0 1.4 fusion.33
  75.4 1.5 fusion.35
  76.9 1.5 fusion.31
  78.4 2.4 fusion.39
  80.7 2.0 subtract_exponential_fusion.1
  82.8 2.1 subtract_exponential_fusion.3
  84.9 2.1 subtract_exponential_fusion.2
  86.9 2.0 subtract_exponential_fusion.4
  88.9 2.0 subtract_exponential_fusion
  90.9 11.9 %convolution_convert_fusion = bf16[1024,640]{0,1:T(8,128)(2,1)S(1)} fusion(bf16[1024,5120]{1,0:T(8,128)(2,1)} %all-gather.2.cloned.1.call-done, bf16[640,5120]{1,0:T(8,128)(2,1)} %param.49), kind=kOutput, calls=%fused_computation.35 | convolution fusion | flops 6711541760 | bytes 18350080 | tf_op jit(solution)/shard_map/dot_general | solution.py:53
  103.3 1.1 copy-done.4
  104.4 0.5 multiply_convert_fusion.4
  104.9 0.4 convolution_convert_fusion.10
  105.4 0.5 fusion.149
  110.5 14.2 %fusion.218 = f32[640,5120]{1,0:T(8,128)} fusion(bf16[1024,640]{0,1:T(8,128)(2,1)S(1)} %bitcast.489, bf16[1024,5120]{1,0:T(8,128)(2,1)} %all-gather.2.cloned.1.call-done), kind=kOutput, calls=%fused_computation.328 | convolution fusion | flops 6710886400 | bytes 24903680 | tf_op jit(solution)/shard_map/dot_general | solution.py:47
  124.7 0.5 multiply_convert_fusion.1
  125.2 0.4 convolution_convert_fusion.7
  125.6 0.6 copy-done.3
  126.3 0.5 multiply_convert_fusion.3
  126.8 0.4 convolution_convert_fusion.9
  127.2 0.6 copy-done.2
  127.8 0.5 multiply_convert_fusion.2
  128.3 0.4 convolution_convert_fusion.8
  128.8 0.5 fusion.61
  129.7 0.5 fusion.62
  130.5 0.5 fusion.63
  131.4 0.5 fusion.64
  133.0 0.5 fusion.57
  133.5 0.4 fusion.73
  133.9 0.5 fusion.58
  134.4 0.4 fusion.75
  134.8 0.5 fusion.59
  135.3 0.4 fusion.77
  135.7 0.7 copy-done
  136.4 0.5 fusion.71
  136.9 0.5 multiply_convert_fusion
  137.4 0.4 convolution_convert_fusion.6
  137.8 0.5 fusion.70
  138.8 2.5 copy.45
  141.3 2.0 copy.56
  143.3 1.5 copy.46
  144.9 5.3 %all-to-all-start.1 = ((bf16[8,128,896]{1,2,0:T(8,128)(2,1)}), bf16[8,128,896]{1,2,0:T(8,128)(2,1)S(1)}, u32[]{:S(2)}, u32[]{:S(2)}) async-start(bf16[8,128,896]{1,2,0:T(8,128)(2,1)} %copy.46), calls=%async_computation.1 | async-start | bytes 3670016 | tf_op jit(solution)/shard_map/all_to_all | solution.py:170
  150.1 289.2 %all-reduce.2 = bf16[640,5120]{1,0:T(8,128)(2,1)} all-reduce(f32[640,5120]{1,0:T(8,128)} %fusion.218), channel_id=1, replica_groups=mesh['leaf'=16,'ctx'=8] {'leaf'}, use_global_device_ids=true, to_apply=%region_17.18 | all-reduce | flops 3276800 | bytes 19660800 | tf_op jit(solution)/shard_map/psum | solution.py:112
  439.3 2.9 copy.47
  (99 shorter events, 10.3 us)
Async XLA Ops:
  7.2 83.8 %all-gather.2.cloned.1.call-start = ((), (), s32[]{:S(2)}) async-start(), calls=%async_computation.2 | async-start | bytes 11796480 | tf_op jit(solution)/shard_map/all_gather | solution.py:108
  11.8 5.9 %copy-start.16 = (s32[1,8]{1,0:T(1,128)S(1)}, s32[1,8]{1,0:T(1,128)}, u32[]{:S(2)}) copy-start(s32[1,8]{1,0:T(1,128)} %param.50) | copy-start | bytes 100
  11.8 42.6 %all-to-all-start = ((bf16[128,8,896]{0,2,1:T(8,128)(2,1)}), bf16[128,8,896]{0,2,1:T(8,128)(2,1)S(1)}, u32[]{:S(2)}, u32[]{:S(2)}) async-start(bf16[128,8,896]{0,2,1:T(8,128)(2,1)} %bitcast.482), calls=%async_computation | async-start | bytes 3670016 | tf_op jit(solution)/shard_map/all_to_all | solution.py:60
  21.6 4.3 copy-start.15
  21.9 53.5 %copy-start.14 = (pred[512,512]{1,0:T(32,128)(4,1)}, pred[512,512]{1,0:T(32,128)(4,1)S(1)}, u32[]{:S(2)}) copy-start(pred[512,512]{1,0:T(32,128)(4,1)S(1)} %fusion.92) | copy-start | bytes 786436
  67.6 3.6 copy-start.11
  71.2 2.7 copy-start.9
  90.9 11.9 %copy-start.12 = (bf16[512,1,5,128]{0,3,2,1:T(8,128)(2,1)S(1)}, bf16[512,1,5,128]{0,3,2,1:T(8,128)(2,1)}, u32[]{:S(2)}) copy-start(bf16[512,1,5,128]{0,3,2,1:T(8,128)(2,1)} %copy-done.11) | copy-start | bytes 1966084
  90.9 12.1 %copy-start.10 = (bf16[512,1,5,128]{0,3,2,1:T(8,128)(2,1)S(1)}, bf16[512,1,5,128]{0,3,2,1:T(8,128)(2,1)}, u32[]{:S(2)}) copy-start(bf16[512,1,5,128]{0,3,2,1:T(8,128)(2,1)} %copy-done.9) | copy-start | bytes 1966084
  102.8 1.6 copy-start.4
  104.9 1.2 copy-start.5
  105.4 1.4 copy-start.8
  106.5 1.3 copy-start.7
  108.4 1.2 copy-start.6
  109.1 1.4 copy-start.13
  110.5 14.2 %copy-start.1 = (f32[512,1024]{1,0:T(8,128)S(1)}, f32[512,1024]{1,0:T(8,128)}, u32[]{:S(2)}) copy-start(f32[512,1024]{1,0:T(8,128)} %subtract_exponential_fusion.1) | copy-start | bytes 6291460
  124.7 1.6 copy-start.3
  126.3 1.6 copy-start.2
  134.8 1.6 copy-start
  144.9 294.5 %all-to-all-start.1 = ((bf16[8,128,896]{1,2,0:T(8,128)(2,1)}), bf16[8,128,896]{1,2,0:T(8,128)(2,1)S(1)}, u32[]{:S(2)}, u32[]{:S(2)}) async-start(bf16[8,128,896]{1,2,0:T(8,128)(2,1)} %copy.46), calls=%async_computation.1 | async-start | bytes 3670016 | tf_op jit(solution)/shard_map/all_to_all | solution.py:170
Sparse Core Ops, SparseCore 0:
  9.7 75.9 all-gather.1
where the time goes:
time: 454 us; the launch traced here: 449 us
  blocking collectives  289 us (64%)
  matrix products  68.7 us (15%)
  waiting for transfers between devices  29.2 us (6%)
  local copies, waits for them, and re-layouts  27.2 us (6%)
  between operations  14.9 us (3%)
  starting transfers between devices  11.2 us (2%)
  other arithmetic  8.76 us (2%)
    psum x1, blocking collectives, local(): weight_total = lax.psum(weight_acc, 'leaf').astype(jnp.bfloat16)  289 us
    dot_general x21, matrix products, contract_cols(): lax.dot_general(left, right, (((1,), (1,)), ((), ())), preferred_element_...  34.4 us
    all_to_all x1, waiting for transfers between devices, local(): lax.all_to_all(query_key_value_rows, 'ctx', split_axis=1, concat_axis=0,...  28.5 us
    dot_general x21, matrix products, contract_rows(): lax.dot_general(left, right, (((0,), (0,)), ((), ())), preferred_element_...  22.7 us
    unnamed x38, local copies, waits for them, and re-layouts  13 us
  transfers between devices with their start and end apart: 3, of which 1 were waited for; matrix products, arithmetic and copies ran while one was open for 11% of the time, Pallas kernels for 0%

commit v1 on v0

--- a/solution.py
+++ b/solution.py
@@ -109,7 +109,8 @@
     weight_acc = contract_rows(flat_out, shard_rows)
     local_grad = contract_cols(shard_rows, out_weight).astype(jnp.bfloat16)
     weight_acc, output_gradient = (weight_acc, local_grad)
-    weight_total = lax.psum(weight_acc, "leaf").astype(jnp.bfloat16)
+    weight_part = lax.psum_scatter(weight_acc, "leaf", scatter_dimension=0, tiled=True)
+    weight_total = lax.all_gather(weight_part.astype(jnp.bfloat16), "leaf", axis=0, tiled=True)
     key_acc = jnp.zeros((tree_len, kv_local, HEAD_SIZE), jnp.float32)
     value_acc = jnp.zeros((tree_len, kv_local, HEAD_SIZE), jnp.float32)
     query_parts = []

time: 454 us -> 276 us (0.61)
  blocking collectives: 289 us -> 28.6 us
  waiting for transfers between devices: 29.2 us -> 112 us
  local copies, waits for them, and re-layouts: 27.2 us -> 34.1 us
  starting transfers between devices: 11.2 us -> 6.23 us
    psum x1 -> x0, blocking collectives: 289 us -> none  [local(): weight_total = lax.psum(weight_acc, 'leaf').astype(jnp.bfloat16)]
    unnamed x1 -> x4, waiting for transfers between devices: 0.68 us -> 68.7 us
    all_to_all x0 -> x1, blocking collectives: none -> 28.6 us  [local(): lax.all_to_all(gradients, 'ctx', split_axis=0, concat_axis=1, tiled=True)]
    all_gather x1, waiting for transfers between devices: 0.01 us -> 12.9 us  [local(): shard_rows = lax.all_gather(cotangent, 'ctx', axis=0, tiled=True)]
    unnamed x38 -> x51, local copies, waits for them, and re-layouts: 13 us -> 21.3 us
    all_to_all x1 -> x0, starting transfers between devices: 5.26 us -> none  [local(): lax.all_to_all(gradients, 'ctx', split_axis=0, concat_axis=1, tiled=True)]
  transfers between devices with their start and end apart: 3 -> 4, of which waited for: 1 -> 4; matrix products, arithmetic and copies ran while one was open for 11% -> 30% of each run, Pallas kernels for 0% -> 0%
where the time goes in v1:
time: 276 us; the launch traced here: 271 us
  waiting for transfers between devices  112 us (41%)
  matrix products  64.7 us (23%)
  local copies, waits for them, and re-layouts  34.1 us (12%)
  blocking collectives  28.6 us (10%)
  between operations  14.6 us (5%)
  other arithmetic  10.7 us (4%)
  starting transfers between devices  6.23 us (2%)
    unnamed x4, waiting for transfers between devices  68.7 us
    dot_general x21, matrix products, contract_cols(): lax.dot_general(left, right, (((1,), (1,)), ((), ())), preferred_element_...  30.7 us
    all_to_all x1, blocking collectives, local(): lax.all_to_all(gradients, 'ctx', split_axis=0, concat_axis=1, tiled=True)  28.6 us
    all_to_all x1, waiting for transfers between devices, local(): lax.all_to_all(query_key_value_rows, 'ctx', split_axis=1, concat_axis=0,...  28.5 us
    dot_general x21, matrix products, contract_rows(): lax.dot_general(left, right, (((0,), (0,)), ((), ())), preferred_element_...  22.8 us
    unnamed x51, local copies, waits for them, and re-layouts  21.3 us
    all_gather x1, waiting for transfers between devices, local(): shard_rows = lax.all_gather(cotangent, 'ctx', axis=0, tiled=True)  12.9 us
    all_to_all x1, starting transfers between devices, local(): lax.all_to_all(query_key_value_rows, 'ctx', split_axis=1, concat_axis=0,...  5.93 us
  transfers between devices with their start and end apart: 4, of which 4 were waited for; matrix products, arithmetic and copies ran while one was open for 30% of the time, Pallas kernels for 0%

profile of v1, /device:TPU:1, one launch (start us, length us, event | category | flops | bytes accessed | tf_op | source)
XLA Modules:
  0.0 271.4 jit_solution(1892407412926653533)
XLA Ops:
  7.2 0.7 all-gather.3.cloned.1.call-update
  7.9 3.9 %copy.35 = bf16[128,7168]{0,1:T(8,128)(2,1)} copy(bf16[128,7168]{1,0:T(8,128)(2,1)} %param.47) | data formatting | bytes 3670016 | tf_op args[0]
  11.8 5.9 %all-to-all-start = ((bf16[128,8,896]{0,2,1:T(8,128)(2,1)}), bf16[128,8,896]{0,2,1:T(8,128)(2,1)S(1)}, u32[]{:S(2)}, u32[]{:S(2)}) async-start(bf16[128,8,896]{0,2,1:T(8,128)(2,1)} %bitcast.483), calls=%async_computation | async-start | bytes 3670016 | tf_op jit(solution)/shard_map/all_to_all | solution.py:60
  17.7 2.2 while.34
  20.0 1.6 broadcast_in_dim.71
  22.4 1.6 broadcast_in_dim.76
  24.0 0.8 fusion.14
  24.9 1.0 copy.42
  25.9 28.5 %all-to-all-done = bf16[128,8,896]{0,2,1:T(8,128)(2,1)S(1)} async-done(((bf16[128,8,896]{0,2,1:T(8,128)(2,1)}), bf16[128,8,896]{0,2,1:T(8,128)(2,1)S(1)}, u32[]{:S(2)}, u32[]{:S(2)}) %all-to-all-start) | async-done | bytes 1835040 | tf_op jit(solution)/shard_map/all_to_all | solution.py:60
  54.4 2.4 copy.36
  56.8 2.9 %reshape.966 = bf16[1024,1,7,128]{0,3,2,1:T(8,128)(2,1)S(1)} reshape(bf16[8,128,896]{1,0,2:T(8,128)(2,1)} %copy.36) | data formatting | bytes 3670016 | tf_op jit(solution)/shard_map/reshape | solution.py:64
  59.7 1.0 fusion.8
  60.7 1.1 exponential_reduce_fusion.1
  61.9 1.8 fusion.3
  63.7 2.2 exponential_reduce_fusion
  65.9 1.6 fusion.54
  67.5 3.1 %fusion.51 = bf16[512,1,5,128]{0,3,2,1:T(8,128)(2,1)S(1)} fusion(f32[1024,512,5]{1,0,2:T(8,128)S(1)} %get-tuple-element.332, f32[5,512]{1,0:T(8,128)S(1)} %log_add_fusion, f32[512]{0:T(512)S(1)} %get-tuple-element.330, pred[512,1024]{0,1:T(8,128)(4,1)S(1)} %copy.42, bf16[1024,1,7,128]{0,3,2,1:T(8,128)(2,1)S(1)} %reshape.966), kind=kOutput, calls=%fused_computation.79 | convolution fusion | flops 681902080 | bytes 11945984 | tf_op jit(solution)/shard_map/gjts,sgd->tgjd/dot_general | solution.py:97
  70.6 0.9 copy-done.14
  71.5 1.2 pad_maximum_fusion.1
  72.7 12.9 %all-gather.3.cloned.1.call-done = bf16[1024,5120]{1,0:T(8,128)(2,1)} async-done(((bf16[128,5120]{1,0:T(8,128)(2,1)}), bf16[1024,5120]{1,0:T(8,128)(2,1)}) %all-gather.3.cloned.1.call-update) | async-done | bytes 10485776 | tf_op jit(solution)/shard_map/all_gather | solution.py:108
  85.6 12.7 %fusion.218 = f32[640,5120]{1,0:T(8,128)} fusion(bf16[1024,640]{0,1:T(8,128)(2,1)} %bitcast.490, bf16[1024,5120]{1,0:T(8,128)(2,1)} %all-gather.3.cloned.1.call-done), kind=kOutput, calls=%fused_computation.328 | convolution fusion | flops 6710886400 | bytes 24903680 | tf_op jit(solution)/shard_map/dot_general | solution.py:47
  99.1 1.4 fusion.33
  100.5 1.4 fusion.35
  101.9 1.4 fusion.37
  103.4 1.5 fusion.39
  104.9 0.7 subtract_exponential_fusion.4
  105.5 2.0 subtract_exponential_fusion.3
  107.6 2.0 subtract_exponential_fusion.2
  109.6 2.1 subtract_exponential_fusion.1
  111.7 2.1 subtract_exponential_fusion
  113.8 9.8 %convolution_convert_fusion = bf16[1024,640]{0,1:T(8,128)(2,1)S(1)} fusion(bf16[1024,5120]{1,0:T(8,128)(2,1)S(1)} %bitcast.507, bf16[640,5120]{1,0:T(8,128)(2,1)} %param.49), kind=kOutput, calls=%fused_computation.35 | convolution fusion | flops 6711541760 | bytes 18350080 | tf_op jit(solution)/shard_map/dot_general | solution.py:53
  124.0 1.1 fusion.50
  125.2 1.5 multiply_convert_fusion.4
  126.7 68.0 %reduce-scatter.4.cloned.1.call-done = f32[40,5120]{1,0:T(8,128)} async-done(((f32[640,5120]{1,0:T(8,128)}), f32[40,5120]{1,0:T(8,128)}) %reduce-scatter.4.cloned.1.call-update) | async-done | bytes 819216
  194.7 2.0 convert_element_type.299
  196.7 1.8 fusion.149
  198.9 0.4 convolution_convert_fusion.10
  200.4 0.6 copy-done.3
  201.0 0.5 multiply_convert_fusion.3
  201.5 0.4 convolution_convert_fusion.9
  202.0 0.7 copy-done.11
  203.6 0.5 multiply_convert_fusion.2
  204.1 0.4 convolution_convert_fusion.8
  204.6 0.7 copy-done.10
  206.3 0.5 multiply_convert_fusion.1
  207.3 0.8 copy-done.9
  209.0 0.5 multiply_convert_fusion
  210.0 0.7 copy-done.8
  211.7 0.5 fusion.57
  212.6 0.5 fusion.58
  213.5 0.5 fusion.59
  214.4 0.5 fusion.70
  214.9 0.7 copy-done.5
  215.6 0.5 fusion.61
  216.5 0.7 fusion.62
  217.5 0.5 fusion.63
  218.4 0.5 fusion.64
  219.3 0.5 fusion.71
  220.0 2.5 copy.45
  222.6 2.0 copy.56
  224.8 28.6 %all_to_all.35 = bf16[8,128,896]{1,2,0:T(8,128)(2,1)S(1)} all-to-all(bf16[8,128,896]{1,2,0:T(8,128)(2,1)S(1)} %copy.46), channel_id=1, replica_groups=mesh['leaf'=16,'ctx'=8] {'ctx'}, dimensions={0} | all-to-all | bytes 3670016 | tf_op jit(solution)/shard_map/all_to_all | solution.py:171
  253.5 2.9 %copy.47 = bf16[128,7168]{1,0:T(8,128)(2,1)} copy(bf16[128,7168]{0,1:T(8,128)(2,1)S(1)} %bitcast.486) | data formatting | bytes 3670016
  256.3 2.2 all-gather.5.cloned.1.call-done
  258.6 6.1 %copy.98 = bf16[640,5120]{1,0:T(8,128)(2,1)} copy(bf16[640,5120]{1,0:T(8,128)(2,1)} %all-gather.5.cloned.1.call-done) | data formatting | bytes 13107200
  (118 shorter events, 13.5 us)
Async XLA Ops:
  7.2 78.5 %all-gather.3.cloned.1.call-start = ((), (), s32[]{:S(2)}) async-start(), calls=%async_computation.3 | async-start | bytes 11796480 | tf_op jit(solution)/shard_map/all_gather | solution.py:108
  11.8 6.0 %copy-start.19 = (s32[1,8]{1,0:T(1,128)S(1)}, s32[1,8]{1,0:T(1,128)}, u32[]{:S(2)}) copy-start(s32[1,8]{1,0:T(1,128)} %param.50) | copy-start | bytes 100
  11.8 42.6 %all-to-all-start = ((bf16[128,8,896]{0,2,1:T(8,128)(2,1)}), bf16[128,8,896]{0,2,1:T(8,128)(2,1)S(1)}, u32[]{:S(2)}, u32[]{:S(2)}) async-start(bf16[128,8,896]{0,2,1:T(8,128)(2,1)} %bitcast.483), calls=%async_computation | async-start | bytes 3670016 | tf_op jit(solution)/shard_map/all_to_all | solution.py:60
  17.7 177.0 %reduce-scatter.4.cloned.1.call-start = ((), (), s32[]{:S(2)}) async-start(), calls=%async_computation.5 | async-start | bytes 13926400
  21.6 4.3 %copy-start.18 = (s32[1024]{0:T(1024)S(1)}, s32[1024]{0:T(1024)}, u32[]{:S(2)}) copy-start(s32[1024]{0:T(1024)} %param.51) | copy-start | bytes 12292
  67.5 3.1 %copy-start.16 = (bf16[512,1,5,128]{0,3,2,1:T(8,128)(2,1)}, bf16[512,1,5,128]{0,3,2,1:T(8,128)(2,1)S(1)}, u32[]{:S(2)}) copy-start(bf16[512,1,5,128]{0,3,2,1:T(8,128)(2,1)S(1)} %fusion.54) | copy-start | bytes 1966084
  70.6 0.9 copy-start.14
  98.3 160.2 %all-gather.5.cloned.1.call-start = ((), (), s32[]{:S(2)}) async-start(), calls=%async_computation.4 | async-start | bytes 6963200 | tf_op jit(solution)/shard_map/all_gather | solution.py:113
  99.1 24.9 %copy-start.7 = (f32[512,512]{1,0:T(8,128)}, f32[512,512]{1,0:T(8,128)S(1)}, u32[]{:S(2)}) copy-start(f32[512,512]{1,0:T(8,128)S(1)} %fusion.31) | copy-start | bytes 3145732
  100.5 13.2 %slice-start = ((s8[10485760]{0:T(1024)(128)(4,1)}), s8[4194304]{0:T(1024)(128)(4,1)S(1)}, s32[]{:S(2)}) async-start(s8[10485760]{0:T(1024)(128)(4,1)} %bitcast.506), calls=%async_computation.6 | async-start | bytes 8388608
  104.8 8.9 %slice-start.1 = ((s8[10485760]{0:T(1024)(128)(4,1)}), s8[4194304]{0:T(1024)(128)(4,1)S(1)}, s32[]{:S(2)}) async-start(s8[10485760]{0:T(1024)(128)(4,1)} %bitcast.506), calls=%async_computation.7 | async-start | bytes 8388608
  105.5 19.6 %copy-start.4 = (f32[512,1024]{1,0:T(8,128)}, f32[512,1024]{1,0:T(8,128)S(1)}, u32[]{:S(2)}) copy-start(f32[512,1024]{1,0:T(8,128)S(1)} %subtract_exponential_fusion.4) | copy-start | bytes 6291460
  107.5 6.2 %slice-start.2 = ((s8[10485760]{0:T(1024)(128)(4,1)}), s8[2097152]{0:T(1024)(128)(4,1)S(1)}, s32[]{:S(2)}) async-start(s8[10485760]{0:T(1024)(128)(4,1)} %bitcast.506), calls=%async_computation.8 | async-start | bytes 4194304
  113.7 9.8 %copy-start.17 = (bf16[512,1,5,128]{0,3,2,1:T(8,128)(2,1)S(1)}, bf16[512,1,5,128]{0,3,2,1:T(8,128)(2,1)}, u32[]{:S(2)}) copy-start(bf16[512,1,5,128]{0,3,2,1:T(8,128)(2,1)} %copy-done.16) | copy-start | bytes 1966084
  113.7 10.0 %copy-start.15 = (bf16[512,1,5,128]{0,3,2,1:T(8,128)(2,1)S(1)}, bf16[512,1,5,128]{0,3,2,1:T(8,128)(2,1)}, u32[]{:S(2)}) copy-start(bf16[512,1,5,128]{0,3,2,1:T(8,128)(2,1)} %copy-done.14) | copy-start | bytes 1966084
  196.6 1.9 copy-start.6
  196.7 2.2 copy-start.13
  198.5 1.2 copy-start.12
  199.3 1.7 copy-start.3
  201.5 1.2 copy-start.11
  201.9 1.7 copy-start.2
  204.1 1.2 copy-start.10
  204.6 1.8 copy-start.1
  206.8 1.3 copy-start.9
  207.3 1.7 copy-start
  209.5 1.2 copy-start.8
  214.0 1.6 copy-start.5
Sparse Core Ops, SparseCore 0:
  9.7 75.9 all-gather.2
  98.5 96.1 reduce-scatter.3
  197.1 61.4 all-gather.4

commit v2 on v0

--- a/solution.py
+++ b/solution.py
@@ -109,7 +109,10 @@
     weight_acc = contract_rows(flat_out, shard_rows)
     local_grad = contract_cols(shard_rows, out_weight).astype(jnp.bfloat16)
     weight_acc, output_gradient = (weight_acc, local_grad)
-    weight_total = lax.psum(weight_acc, "leaf").astype(jnp.bfloat16)
+    weight_part = lax.psum_scatter(
+        weight_acc.astype(jnp.bfloat16), "leaf", scatter_dimension=0, tiled=True
+    )
+    weight_total = lax.all_gather(weight_part, "leaf", axis=0, tiled=True)
     key_acc = jnp.zeros((tree_len, kv_local, HEAD_SIZE), jnp.float32)
     value_acc = jnp.zeros((tree_len, kv_local, HEAD_SIZE), jnp.float32)
     query_parts = []

time: 454 us -> 262 us (0.58)
  blocking collectives: 289 us -> 29.6 us
  waiting for transfers between devices: 29.2 us -> 99.7 us
  local copies, waits for them, and re-layouts: 27.2 us -> 34 us
  matrix products: 68.7 us -> 63.7 us
  starting transfers between devices: 11.2 us -> 6.23 us
    psum x1 -> x0, blocking collectives: 289 us -> none  [local(): weight_total = lax.psum(weight_acc, 'leaf').astype(jnp.bfloat16)]
    unnamed x1 -> x4, waiting for transfers between devices: 0.68 us -> 53.7 us
    all_to_all x0 -> x1, blocking collectives: none -> 29.6 us  [local(): lax.all_to_all(gradients, 'ctx', split_axis=0, concat_axis=1, tiled=True)]
    all_gather x1, waiting for transfers between devices: 0.01 us -> 12.9 us  [local(): shard_rows = lax.all_gather(cotangent, 'ctx', axis=0, tiled=True)]
    unnamed x38 -> x51, local copies, waits for them, and re-layouts: 13 us -> 21.3 us
    all_to_all x1 -> x0, starting transfers between devices: 5.26 us -> none  [local(): lax.all_to_all(gradients, 'ctx', split_axis=0, concat_axis=1, tiled=True)]
    all_gather x0 -> x1, waiting for transfers between devices: none -> 4.62 us  [local(): weight_total = lax.all_gather(weight_part, 'leaf', axis=0, tiled=True)]
  transfers between devices with their start and end apart: 3 -> 4, of which waited for: 1 -> 4; matrix products, arithmetic and copies ran while one was open for 11% -> 32% of each run, Pallas kernels for 0% -> 0%
where the time goes in v2:
time: 262 us; the launch traced here: 257 us
  waiting for transfers between devices  99.7 us (38%)
  matrix products  63.7 us (24%)
  local copies, waits for them, and re-layouts  34 us (13%)
  blocking collectives  29.6 us (11%)
  between operations  14.6 us (6%)
  other arithmetic  8.72 us (3%)
  starting transfers between devices  6.23 us (2%)
    unnamed x4, waiting for transfers between devices  53.7 us
    dot_general x21, matrix products, contract_cols(): lax.dot_general(left, right, (((1,), (1,)), ((), ())), preferred_element_...  30.6 us
    all_to_all x1, blocking collectives, local(): lax.all_to_all(gradients, 'ctx', split_axis=0, concat_axis=1, tiled=True)  29.6 us
    all_to_all x1, waiting for transfers between devices, local(): lax.all_to_all(query_key_value_rows, 'ctx', split_axis=1, concat_axis=0,...  28.5 us
    dot_general x21, matrix products, contract_rows(): lax.dot_general(left, right, (((0,), (0,)), ((), ())), preferred_element_...  21.8 us
    unnamed x51, local copies, waits for them, and re-layouts  21.3 us
    all_gather x1, waiting for transfers between devices, local(): shard_rows = lax.all_gather(cotangent, 'ctx', axis=0, tiled=True)  12.9 us
    all_to_all x1, starting transfers between devices, local(): lax.all_to_all(query_key_value_rows, 'ctx', split_axis=1, concat_axis=0,...  5.93 us
  transfers between devices with their start and end apart: 4, of which 4 were waited for; matrix products, arithmetic and copies ran while one was open for 32% of the time, Pallas kernels for 0%

profile of v2, /device:TPU:1, one launch (start us, length us, event | category | flops | bytes accessed | tf_op | source)
XLA Modules:
  0.0 256.6 jit_solution(4817943319971196910)
XLA Ops:
  7.2 0.7 all-gather.3.cloned.1.call-update
  7.9 3.9 %copy.35 = bf16[128,7168]{0,1:T(8,128)(2,1)} copy(bf16[128,7168]{1,0:T(8,128)(2,1)} %param.47) | data formatting | bytes 3670016 | tf_op args[0]
  11.8 5.9 %all-to-all-start = ((bf16[128,8,896]{0,2,1:T(8,128)(2,1)}), bf16[128,8,896]{0,2,1:T(8,128)(2,1)S(1)}, u32[]{:S(2)}, u32[]{:S(2)}) async-start(bf16[128,8,896]{0,2,1:T(8,128)(2,1)} %bitcast.483), calls=%async_computation | async-start | bytes 3670016 | tf_op jit(solution)/shard_map/all_to_all | solution.py:60
  17.7 2.2 while.34
  20.0 1.6 broadcast_in_dim.71
  22.4 1.6 broadcast_in_dim.76
  24.0 0.8 fusion.14
  24.9 1.0 copy.42
  25.9 28.5 %all-to-all-done = bf16[128,8,896]{0,2,1:T(8,128)(2,1)S(1)} async-done(((bf16[128,8,896]{0,2,1:T(8,128)(2,1)}), bf16[128,8,896]{0,2,1:T(8,128)(2,1)S(1)}, u32[]{:S(2)}, u32[]{:S(2)}) %all-to-all-start) | async-done | bytes 1835040 | tf_op jit(solution)/shard_map/all_to_all | solution.py:60
  54.4 2.4 copy.36
  56.8 2.9 %reshape.966 = bf16[1024,1,7,128]{0,3,2,1:T(8,128)(2,1)S(1)} reshape(bf16[8,128,896]{1,0,2:T(8,128)(2,1)} %copy.36) | data formatting | bytes 3670016 | tf_op jit(solution)/shard_map/reshape | solution.py:64
  59.7 1.0 fusion.8
  60.7 1.1 exponential_reduce_fusion.1
  61.9 1.8 fusion.3
  63.7 2.2 exponential_reduce_fusion
  65.9 1.6 fusion.54
  67.5 3.1 %fusion.51 = bf16[512,1,5,128]{0,3,2,1:T(8,128)(2,1)S(1)} fusion(f32[1024,512,5]{1,0,2:T(8,128)S(1)} %get-tuple-element.332, f32[5,512]{1,0:T(8,128)S(1)} %log_add_fusion, f32[512]{0:T(512)S(1)} %get-tuple-element.330, pred[512,1024]{0,1:T(8,128)(4,1)S(1)} %copy.42, bf16[1024,1,7,128]{0,3,2,1:T(8,128)(2,1)S(1)} %reshape.966), kind=kOutput, calls=%fused_computation.80 | convolution fusion | flops 681902080 | bytes 11945984 | tf_op jit(solution)/shard_map/gjts,sgd->tgjd/dot_general | solution.py:97
  70.6 0.9 copy-done.14
  71.5 1.2 pad_maximum_fusion.1
  72.7 12.9 %all-gather.3.cloned.1.call-done = bf16[1024,5120]{1,0:T(8,128)(2,1)} async-done(((bf16[128,5120]{1,0:T(8,128)(2,1)}), bf16[1024,5120]{1,0:T(8,128)(2,1)}) %all-gather.3.cloned.1.call-update) | async-done | bytes 10485776 | tf_op jit(solution)/shard_map/all_gather | solution.py:108
  85.6 11.7 %convolution_convert_fusion = bf16[640,5120]{1,0:T(8,128)(2,1)} fusion(bf16[1024,640]{0,1:T(8,128)(2,1)} %bitcast.490, bf16[1024,5120]{1,0:T(8,128)(2,1)} %all-gather.3.cloned.1.call-done), kind=kOutput, calls=%fused_computation.10 | convolution fusion | flops 6714163200 | bytes 18350080 | tf_op jit(solution)/shard_map/dot_general | solution.py:47
  97.7 1.4 fusion.37
  99.1 1.4 fusion.33
  100.5 1.4 fusion.35
  102.4 1.5 fusion.39
  103.9 2.0 subtract_exponential_fusion.1
  105.9 2.0 subtract_exponential_fusion.3
  107.9 2.0 subtract_exponential_fusion.2
  109.9 0.7 subtract_exponential_fusion.4
  110.6 2.0 subtract_exponential_fusion
  112.7 9.8 %convolution_convert_fusion.1 = bf16[1024,640]{0,1:T(8,128)(2,1)S(1)} fusion(bf16[1024,5120]{1,0:T(8,128)(2,1)S(1)} %bitcast.507, bf16[640,5120]{1,0:T(8,128)(2,1)} %param.49), kind=kOutput, calls=%fused_computation.36 | convolution fusion | flops 6711541760 | bytes 18350080 | tf_op jit(solution)/shard_map/dot_general | solution.py:53
  122.9 1.1 fusion.50
  124.1 1.5 multiply_convert_fusion.4
  125.6 53.0 %reduce-scatter.4.cloned.1.call-done = bf16[40,5120]{1,0:T(8,128)(2,1)} async-done(((bf16[640,5120]{1,0:T(8,128)(2,1)}), bf16[40,5120]{1,0:T(8,128)(2,1)}) %reduce-scatter.4.cloned.1.call-update) | async-done | bytes 409616
  178.6 1.8 fusion.149
  180.8 0.4 convolution_convert_fusion.11
  182.3 0.6 copy-done.3
  182.9 0.5 multiply_convert_fusion.3
  183.4 0.4 convolution_convert_fusion.10
  183.9 0.7 copy-done.11
  185.5 0.5 multiply_convert_fusion.2
  186.0 0.4 convolution_convert_fusion.9
  186.5 0.7 copy-done.9
  188.2 0.5 multiply_convert_fusion.1
  188.7 0.4 convolution_convert_fusion.8
  189.2 0.7 copy-done.10
  190.8 0.5 multiply_convert_fusion
  191.8 0.8 copy-done.8
  193.6 0.5 fusion.57
  194.5 0.5 fusion.58
  195.4 0.5 fusion.59
  196.2 0.5 fusion.70
  196.7 0.7 copy-done.5
  197.5 0.5 fusion.61
  198.3 0.7 fusion.62
  199.4 0.5 fusion.63
  200.3 0.5 fusion.64
  201.2 0.5 fusion.71
  201.9 2.5 copy.45
  204.5 2.0 copy.56
  206.7 29.6 %all_to_all.35 = bf16[8,128,896]{1,2,0:T(8,128)(2,1)S(1)} all-to-all(bf16[8,128,896]{1,2,0:T(8,128)(2,1)S(1)} %copy.46), channel_id=1, replica_groups=mesh['leaf'=16,'ctx'=8] {'ctx'}, dimensions={0} | all-to-all | bytes 3670016 | tf_op jit(solution)/shard_map/all_to_all | solution.py:173
  236.4 2.9 %copy.47 = bf16[128,7168]{1,0:T(8,128)(2,1)} copy(bf16[128,7168]{0,1:T(8,128)(2,1)S(1)} %bitcast.486) | data formatting | bytes 3670016
  239.2 4.6 %all-gather.5.cloned.1.call-done = bf16[640,5120]{1,0:T(8,128)(2,1)} async-done(((bf16[40,5120]{1,0:T(8,128)(2,1)}), bf16[640,5120]{1,0:T(8,128)(2,1)}) %all-gather.5.cloned.1.call-update) | async-done | bytes 6553616 | tf_op jit(solution)/shard_map/all_gather | solution.py:115
  243.8 6.1 %copy.98 = bf16[640,5120]{1,0:T(8,128)(2,1)} copy(bf16[640,5120]{1,0:T(8,128)(2,1)} %all-gather.5.cloned.1.call-done) | data formatting | bytes 13107200
  (117 shorter events, 13.0 us)
Async XLA Ops:
  7.2 78.5 %all-gather.3.cloned.1.call-start = ((), (), s32[]{:S(2)}) async-start(), calls=%async_computation.3 | async-start | bytes 11796480 | tf_op jit(solution)/shard_map/all_gather | solution.py:108
  11.8 6.0 %copy-start.19 = (s32[1,8]{1,0:T(1,128)S(1)}, s32[1,8]{1,0:T(1,128)}, u32[]{:S(2)}) copy-start(s32[1,8]{1,0:T(1,128)} %param.50) | copy-start | bytes 100
  11.8 42.6 %all-to-all-start = ((bf16[128,8,896]{0,2,1:T(8,128)(2,1)}), bf16[128,8,896]{0,2,1:T(8,128)(2,1)S(1)}, u32[]{:S(2)}, u32[]{:S(2)}) async-start(bf16[128,8,896]{0,2,1:T(8,128)(2,1)} %bitcast.483), calls=%async_computation | async-start | bytes 3670016 | tf_op jit(solution)/shard_map/all_to_all | solution.py:60
  17.7 160.8 %reduce-scatter.4.cloned.1.call-start = ((), (), s32[]{:S(2)}) async-start(), calls=%async_computation.5 | async-start | bytes 6963200
  21.6 4.3 %copy-start.18 = (s32[1024]{0:T(1024)S(1)}, s32[1024]{0:T(1024)}, u32[]{:S(2)}) copy-start(s32[1024]{0:T(1024)} %param.51) | copy-start | bytes 12292
  67.5 3.1 %copy-start.16 = (bf16[512,1,5,128]{0,3,2,1:T(8,128)(2,1)}, bf16[512,1,5,128]{0,3,2,1:T(8,128)(2,1)S(1)}, u32[]{:S(2)}) copy-start(bf16[512,1,5,128]{0,3,2,1:T(8,128)(2,1)S(1)} %fusion.54) | copy-start | bytes 1966084
  70.6 0.9 copy-start.14
  97.4 146.5 %all-gather.5.cloned.1.call-start = ((), (), s32[]{:S(2)}) async-start(), calls=%async_computation.4 | async-start | bytes 6963200 | tf_op jit(solution)/shard_map/all_gather | solution.py:115
  100.5 12.2 %slice-start = ((s8[10485760]{0:T(1024)(128)(4,1)}), s8[4194304]{0:T(1024)(128)(4,1)S(1)}, s32[]{:S(2)}) async-start(s8[10485760]{0:T(1024)(128)(4,1)} %bitcast.506), calls=%async_computation.6 | async-start | bytes 8388608
  102.4 20.5 %copy-start.7 = (f32[512,512]{1,0:T(8,128)}, f32[512,512]{1,0:T(8,128)S(1)}, u32[]{:S(2)}) copy-start(f32[512,512]{1,0:T(8,128)S(1)} %fusion.31) | copy-start | bytes 3145732
  103.9 8.8 %slice-start.1 = ((s8[10485760]{0:T(1024)(128)(4,1)}), s8[4194304]{0:T(1024)(128)(4,1)S(1)}, s32[]{:S(2)}) async-start(s8[10485760]{0:T(1024)(128)(4,1)} %bitcast.506), calls=%async_computation.7 | async-start | bytes 8388608
  107.9 4.8 %slice-start.2 = ((s8[10485760]{0:T(1024)(128)(4,1)}), s8[2097152]{0:T(1024)(128)(4,1)S(1)}, s32[]{:S(2)}) async-start(s8[10485760]{0:T(1024)(128)(4,1)} %bitcast.506), calls=%async_computation.8 | async-start | bytes 4194304
  110.6 13.5 %copy-start.4 = (f32[512,1024]{1,0:T(8,128)}, f32[512,1024]{1,0:T(8,128)S(1)}, u32[]{:S(2)}) copy-start(f32[512,1024]{1,0:T(8,128)S(1)} %subtract_exponential_fusion.4) | copy-start | bytes 6291460
  112.7 9.8 %copy-start.17 = (bf16[512,1,5,128]{0,3,2,1:T(8,128)(2,1)S(1)}, bf16[512,1,5,128]{0,3,2,1:T(8,128)(2,1)}, u32[]{:S(2)}) copy-start(bf16[512,1,5,128]{0,3,2,1:T(8,128)(2,1)} %copy-done.16) | copy-start | bytes 1966084
  112.7 10.0 %copy-start.15 = (bf16[512,1,5,128]{0,3,2,1:T(8,128)(2,1)S(1)}, bf16[512,1,5,128]{0,3,2,1:T(8,128)(2,1)}, u32[]{:S(2)}) copy-start(bf16[512,1,5,128]{0,3,2,1:T(8,128)(2,1)} %copy-done.14) | copy-start | bytes 1966084
  178.6 1.9 copy-start.6
  178.6 2.2 copy-start.13
  180.4 1.2 copy-start.12
  181.2 1.7 copy-start.3
  183.4 1.2 copy-start.11
  183.9 1.7 copy-start.2
  186.0 1.2 copy-start.9
  186.5 1.7 copy-start
  188.7 1.2 copy-start.10
  189.1 1.7 copy-start.1
  191.3 1.3 copy-start.8
  195.9 1.6 copy-start.5
Sparse Core Ops, SparseCore 0:
  9.7 75.9 all-gather.2
  97.5 81.0 reduce-scatter.3
  181.0 62.8 all-gather.4

commit v3 on v2

--- a/solution.py
+++ b/solution.py
@@ -53,6 +53,34 @@
     return lax.dot_general(
         left, right, (((1,), (1,)), ((), ())), preferred_element_type=jnp.float32
     )
+
+
+def gather_tree_rows(rows):
+    cores = 2
+    chips = lax.axis_size("ctx") // cores
+    me = lax.axis_index("ctx")
+    my_chip = me // cores
+    my_core = me % cores
+    blocks = [rows]
+    chip_of = [my_chip]
+    for shift in range(1, chips):
+        pairs = [
+            (chip * cores + core, ((chip + shift) % chips) * cores + core)
+            for chip in range(chips)
+            for core in range(cores)
+        ]
+        blocks.append(lax.ppermute(rows, "ctx", pairs))
+        chip_of.append((my_chip - shift) % chips)
+    mine = jnp.stack(blocks)
+    swap = [(chip * cores + core, chip * cores + 1 - core) for chip in range(chips) for core in range(cores)]
+    theirs = lax.ppermute(mine, "ctx", swap)
+    block_len = rows.shape[0]
+    full = jnp.zeros((chips * cores * block_len, rows.shape[1]), rows.dtype)
+    for slot in range(chips):
+        for core, source in ((my_core, mine), (1 - my_core, theirs)):
+            start = (chip_of[slot] * cores + core) * block_len
+            full = lax.dynamic_update_slice(full, source[slot], (start, 0))
+    return full
 
 
 def local(query_key_value_rows, cotangent, out_weight, parents, rollout_spans):
@@ -105,7 +133,7 @@
     attended = jnp.concatenate(attended_parts, axis=0)
     log_totals = jnp.concatenate(total_parts, axis=2)
     flat_out = attended.reshape(tree_len, heads_local * HEAD_SIZE)
-    shard_rows = lax.all_gather(cotangent, "ctx", axis=0, tiled=True)
+    shard_rows = gather_tree_rows(cotangent)
     weight_acc = contract_rows(flat_out, shard_rows)
     local_grad = contract_cols(shard_rows, out_weight).astype(jnp.bfloat16)
     weight_acc, output_gradient = (weight_acc, local_grad)

time: 262 us -> 301 us (1.15)
  local copies, waits for them, and re-layouts: 34 us -> 56.3 us
  starting transfers between devices: 6.23 us -> 13.5 us
  other arithmetic: 8.72 us -> 13.6 us
  waiting for transfers between devices: 99.7 us -> 103 us
    ppermute x0 -> x4, waiting for transfers between devices: none -> 40.4 us  [the longest x3 40.4 us: gather_tree_rows(): blocks.append(lax.ppermute(rows, 'ctx', pairs))]
    all_to_all x1, waiting for transfers between devices: 28.5 us -> 1.42 us  [local(): lax.all_to_all(query_key_value_rows, 'ctx', split_axis=1, concat_axis=0,...]
    dynamic_update_slice x0 -> x8, local copies, waits for them, and re-layouts: none -> 18.6 us  [gather_tree_rows(): full = lax.dynamic_update_slice(full, source[slot], (start, 0))]
    all_gather x1 -> x0, waiting for transfers between devices: 12.9 us -> none  [local(): shard_rows = lax.all_gather(cotangent, 'ctx', axis=0, tiled=True)]
    ppermute x0 -> x4, starting transfers between devices: none -> 8.29 us  [the longest x3 5.71 us: gather_tree_rows(): blocks.append(lax.ppermute(rows, 'ctx', pairs))]
    broadcast_in_dim x0 -> x1, local copies, waits for them, and re-layouts: none -> 5.29 us  [gather_tree_rows(): full = jnp.zeros((chips * cores * block_len, rows.shape[1]), rows.dtype)]
    another operation x0 -> x1, other arithmetic: none -> 5.17 us  [gather_tree_rows(): mine = jnp.stack(blocks)]
    unnamed x51 -> x55, local copies, waits for them, and re-layouts: 21.3 us -> 18.9 us
  transfers between devices with their start and end apart: 4 -> 7, of which waited for: 4 -> 6; matrix products, arithmetic and copies ran while one was open for 32% -> 32% of each run, Pallas kernels for 0% -> 0%
where the time goes in v3:
time: 301 us; the launch traced here: 297 us
  waiting for transfers between devices  103 us (34%)
  matrix products  65.5 us (22%)
  local copies, waits for them, and re-layouts  56.3 us (19%)
  blocking collectives  29.5 us (10%)
  between operations  15 us (5%)
  other arithmetic  13.6 us (5%)
  starting transfers between devices  13.5 us (4%)
    unnamed x3, waiting for transfers between devices  54.5 us
    ppermute x3, waiting for transfers between devices, gather_tree_rows(): blocks.append(lax.ppermute(rows, 'ctx', pairs))  40.4 us
    dot_general x21, matrix products, contract_cols(): lax.dot_general(left, right, (((1,), (1,)), ((), ())), preferred_element_...  30.9 us
    all_to_all x1, blocking collectives, local(): lax.all_to_all(gradients, 'ctx', split_axis=0, concat_axis=1, tiled=True)  29.5 us
    dot_general x21, matrix products, contract_rows(): lax.dot_general(left, right, (((0,), (0,)), ((), ())), preferred_element_...  23 us
    unnamed x55, local copies, waits for them, and re-layouts  18.9 us
    dynamic_update_slice x8, local copies, waits for them, and re-layouts, gather_tree_rows(): full = lax.dynamic_update_slice(full, source[slot], (start, 0))  18.6 us
    all_gather x1, waiting for transfers between devices, local(): weight_total = lax.all_gather(weight_part, 'leaf', axis=0, tiled=True)  6.98 us
  transfers between devices with their start and end apart: 7, of which 6 were waited for; matrix products, arithmetic and copies ran while one was open for 32% of the time, Pallas kernels for 0%

profile of v3, /device:TPU:1, one launch (start us, length us, event | category | flops | bytes accessed | tf_op | source)
XLA Modules:
  0.0 296.9 jit_solution(6859515300666879728)
XLA Ops:
  7.2 2.1 collective-permute-start
  9.3 2.5 collective-permute-start.1
  11.7 1.2 collective-permute-start.2
  12.9 3.9 %copy.35 = bf16[128,7168]{0,1:T(8,128)(2,1)} copy(bf16[128,7168]{1,0:T(8,128)(2,1)} %param.47) | data formatting | bytes 3670016 | tf_op args[0]
  16.8 5.1 %all-to-all-start = ((bf16[128,8,896]{0,2,1:T(8,128)(2,1)}), bf16[128,8,896]{0,2,1:T(8,128)(2,1)S(1)}, u32[]{:S(2)}, u32[]{:S(2)}) async-start(bf16[128,8,896]{0,2,1:T(8,128)(2,1)} %bitcast.503), calls=%async_computation | async-start | bytes 3670016 | tf_op jit(solution)/shard_map/all_to_all | solution.py:88
  21.9 2.2 while.34
  24.2 1.6 broadcast_in_dim.73
  25.8 1.1 fusion.96
  26.9 1.3 copy.38
  28.2 10.7 %collective-permute-done = bf16[128,5120]{1,0:T(8,128)(2,1)} collective-permute-done((bf16[128,5120]{1,0:T(8,128)(2,1)}, bf16[128,5120]{1,0:T(8,128)(2,1)}, u32[]{:S(2)}, u32[]{:S(2)}) %collective-permute-start) | collective-permute-done | bytes 1310752 | tf_op jit(solution)/shard_map/ppermute | solution.py:72
  38.9 29.4 %collective-permute-done.1 = bf16[128,5120]{1,0:T(8,128)(2,1)} collective-permute-done((bf16[128,5120]{1,0:T(8,128)(2,1)}, bf16[128,5120]{1,0:T(8,128)(2,1)}, u32[]{:S(2)}, u32[]{:S(2)}) %collective-permute-start.1) | collective-permute-done | bytes 1310752 | tf_op jit(solution)/shard_map/ppermute | solution.py:72
  68.7 5.2 %pad_maximum_fusion = bf16[4,128,5120]{2,1,0:T(8,128)(2,1)} fusion(bf16[1,128,5120]{2,1,0:T(8,128)(2,1)} %bitcast.14, bf16[1,128,5120]{2,1,0:T(8,128)(2,1)} %bitcast.13, bf16[1,128,5120]{2,1,0:T(8,128)(2,1)} %bitcast.12, bf16[1,128,5120]{2,1,0:T(8,128)(2,1)S(1)} %bitcast.507), kind=kLoop, calls=%fused_computation.12 | loop fusion | flops 7864320 | bytes 10485760 | tf_op jit(solution)/shard_map/stack | solution.py:74
  73.9 2.6 collective-permute-start.3
  76.5 1.6 broadcast_in_dim.79
  78.1 0.8 fusion.14
  78.9 1.0 copy.42
  80.0 5.3 %broadcast_in_dim.77 = bf16[1024,5120]{1,0:T(8,128)(2,1)} broadcast(bf16[]{:T(256)} %constant.503.clone.1), dimensions={} | broadcast | bytes 10485762 | tf_op jit(solution)/shard_map/broadcast_in_dim | solution.py:78
  85.3 1.2 constant_dynamic-update-slice_fusion.3
  86.5 1.4 all-to-all-done
  87.9 2.4 copy.36
  90.3 2.7 reshape.966
  93.0 1.0 fusion.8
  94.0 1.1 exponential_reduce_fusion.1
  95.2 1.8 fusion.3
  97.0 2.2 exponential_reduce_fusion
  99.2 1.6 fusion.58
  100.8 3.5 %fusion.55 = bf16[512,1,5,128]{0,3,2,1:T(8,128)(2,1)S(1)} fusion(f32[1024,512,5]{1,0,2:T(8,128)S(1)} %get-tuple-element.332, f32[5,512]{1,0:T(8,128)S(1)} %log_add_fusion, f32[512]{0:T(512)S(1)} %get-tuple-element.330, pred[512,1024]{0,1:T(8,128)(4,1)S(1)} %copy.42, bf16[1024,1,7,128]{0,3,2,1:T(8,128)(2,1)S(1)} %reshape.966), kind=kOutput, calls=%fused_computation.89 | convolution fusion | flops 681902080 | bytes 11945984 | tf_op jit(solution)/shard_map/gjts,sgd->tgjd/dot_general | solution.py:125
  104.5 2.5 fusion.49
  107.0 2.4 constant_dynamic-update-slice_fusion.2
  109.5 2.6 fusion.48
  112.0 2.5 constant_dynamic-update-slice_fusion.1
  114.5 2.5 fusion.47
  117.0 2.5 constant_dynamic-update-slice_fusion
  119.5 2.5 fusion.46
  121.9 12.9 %convolution_convert_fusion = bf16[640,5120]{1,0:T(8,128)(2,1)} fusion(bf16[1024,640]{0,1:T(8,128)(2,1)S(1)} %bitcast.511, bf16[1024,5120]{1,0:T(8,128)(2,1)} %fusion.46), kind=kOutput, calls=%fused_computation.10 | convolution fusion | flops 6714163200 | bytes 18350080 | tf_op jit(solution)/shard_map/dot_general | solution.py:47
  134.9 0.8 copy-done.20
  136.2 1.4 fusion.33
  137.6 1.4 fusion.35
  139.1 1.4 fusion.37
  140.5 1.4 fusion.39
  142.0 0.7 subtract_exponential_fusion.4
  142.7 2.0 subtract_exponential_fusion.3
  144.6 2.0 subtract_exponential_fusion.2
  146.7 2.0 subtract_exponential_fusion.1
  148.7 2.0 subtract_exponential_fusion
  150.7 10.1 %convolution_convert_fusion.1 = bf16[1024,640]{0,1:T(8,128)(2,1)S(1)} fusion(bf16[1024,5120]{1,0:T(8,128)(2,1)} %fusion.46, bf16[640,5120]{1,0:T(8,128)(2,1)S(1)} %bitcast.528), kind=kOutput, calls=%fused_computation.37 | convolution fusion | flops 6711541760 | bytes 18350080 | tf_op jit(solution)/shard_map/dot_general | solution.py:53
  161.3 1.2 fusion.54
  162.5 1.5 multiply_convert_fusion.4
  164.0 54.5 %reduce-scatter.4.cloned.1.call-done = bf16[40,5120]{1,0:T(8,128)(2,1)} async-done(((bf16[640,5120]{1,0:T(8,128)(2,1)}), bf16[40,5120]{1,0:T(8,128)(2,1)}) %reduce-scatter.4.cloned.1.call-update) | async-done | bytes 409616
  218.5 1.8 fusion.153
  231.1 0.5 fusion.61
  232.0 0.5 fusion.62
  232.9 0.5 fusion.63
  234.3 0.7 copy-done.5
  235.9 0.7 fusion.66
  237.0 0.5 fusion.67
  237.9 0.5 fusion.68
  238.7 0.5 fusion.75
  239.5 2.5 copy.45
  242.0 2.1 copy.56
  244.3 29.5 %all_to_all.35 = bf16[8,128,896]{1,2,0:T(8,128)(2,1)S(1)} all-to-all(bf16[8,128,896]{1,2,0:T(8,128)(2,1)S(1)} %copy.46), channel_id=1, replica_groups=mesh['leaf'=16,'ctx'=8] {'ctx'}, dimensions={0} | all-to-all | bytes 3670016 | tf_op jit(solution)/shard_map/all_to_all | solution.py:201
  273.9 2.9 copy.47
  276.8 7.0 %all-gather.2.cloned.1.call-done = bf16[640,5120]{1,0:T(8,128)(2,1)} async-done(((bf16[40,5120]{1,0:T(8,128)(2,1)}), bf16[640,5120]{1,0:T(8,128)(2,1)}) %all-gather.2.cloned.1.call-update) | async-done | bytes 6553616 | tf_op jit(solution)/shard_map/all_gather | solution.py:143
  283.7 6.1 %copy.104 = bf16[640,5120]{1,0:T(8,128)(2,1)} copy(bf16[640,5120]{1,0:T(8,128)(2,1)} %all-gather.2.cloned.1.call-done) | data formatting | bytes 13107200
  (136 shorter events, 18.4 us)
Async XLA Ops:
  7.2 31.8 %collective-permute-start = (bf16[128,5120]{1,0:T(8,128)(2,1)}, bf16[128,5120]{1,0:T(8,128)(2,1)}, u32[]{:S(2)}, u32[]{:S(2)}) collective-permute-start(bf16[128,5120]{1,0:T(8,128)(2,1)} %param.48), channel_id=1, source_target_pairs={{0,2},{1,3},{2,4},{3,5},{4,6},{5,7},{6,0},{7,1},{8,10},{9,11},{10,... | collective-permute-start | bytes 3932168 | tf_op jit(solution)/shard_map/ppermute | solution.py:72
  9.3 59.1 %collective-permute-start.1 = (bf16[128,5120]{1,0:T(8,128)(2,1)}, bf16[128,5120]{1,0:T(8,128)(2,1)}, u32[]{:S(2)}, u32[]{:S(2)}) collective-permute-start(bf16[128,5120]{1,0:T(8,128)(2,1)} %param.48), channel_id=1, source_target_pairs={{0,4},{1,5},{2,6},{3,7},{4,0},{5,1},{6,2},{7,3},{8,12},{9,13},{10,... | collective-permute-start | bytes 3932168 | tf_op jit(solution)/shard_map/ppermute | solution.py:72
  11.7 57.0 %collective-permute-start.2 = (bf16[128,5120]{1,0:T(8,128)(2,1)}, bf16[128,5120]{1,0:T(8,128)(2,1)}, u32[]{:S(2)}, u32[]{:S(2)}) collective-permute-start(bf16[128,5120]{1,0:T(8,128)(2,1)} %param.48), channel_id=1, source_target_pairs={{0,6},{1,7},{2,0},{3,1},{4,2},{5,3},{6,4},{7,5},{8,14},{9,15},{10,... | collective-permute-start | bytes 3932168 | tf_op jit(solution)/shard_map/ppermute | solution.py:72
  16.7 5.2 %copy-start.22 = (s32[1,8]{1,0:T(1,128)S(1)}, s32[1,8]{1,0:T(1,128)}, u32[]{:S(2)}) copy-start(s32[1,8]{1,0:T(1,128)} %param.50) | copy-start | bytes 100
  16.7 51.9 %copy-start.6 = (bf16[128,5120]{1,0:T(8,128)(2,1)S(1)}, bf16[128,5120]{1,0:T(8,128)(2,1)}, u32[]{:S(2)}) copy-start(bf16[128,5120]{1,0:T(8,128)(2,1)} %param.48) | copy-start | bytes 3932164
  16.8 71.2 %all-to-all-start = ((bf16[128,8,896]{0,2,1:T(8,128)(2,1)}), bf16[128,8,896]{0,2,1:T(8,128)(2,1)S(1)}, u32[]{:S(2)}, u32[]{:S(2)}) async-start(bf16[128,8,896]{0,2,1:T(8,128)(2,1)} %bitcast.503), calls=%async_computation | async-start | bytes 3670016 | tf_op jit(solution)/shard_map/all_to_all | solution.py:88
  21.9 196.5 %reduce-scatter.4.cloned.1.call-start = ((), (), s32[]{:S(2)}) async-start(), calls=%async_computation.4 | async-start | bytes 6963200
  73.9 6.1 %copy-start.21 = (s32[1024]{0:T(1024)S(1)}, s32[1024]{0:T(1024)}, u32[]{:S(2)}) copy-start(s32[1024]{0:T(1024)} %param.51) | copy-start | bytes 12292
  73.9 30.6 %collective-permute-start.3 = (bf16[4,128,5120]{2,1,0:T(8,128)(2,1)}, bf16[4,128,5120]{2,1,0:T(8,128)(2,1)}, u32[]{:S(2)}, u32[]{:S(2)}) collective-permute-start(bf16[4,128,5120]{2,1,0:T(8,128)(2,1)} %pad_maximum_fusion), channel_id=1, source_target_pairs={{0,1},{1,0},{2,3},{3,2},{4,5},{5,4},{6,7},{7,6},{8,9},{9,8},{10,11... | collective-permute-start | bytes 15728648 | tf_op jit(solution)/shard_map/ppermute | solution.py:76
  80.0 5.3 %copy-start.7 = (bf16[128,5120]{1,0:T(8,128)(2,1)S(1)}, bf16[128,5120]{1,0:T(8,128)(2,1)}, u32[]{:S(2)}) copy-start(bf16[128,5120]{1,0:T(8,128)(2,1)} %param.48) | copy-start | bytes 3932164
  100.8 3.5 %copy-start.18 = (bf16[512,1,5,128]{0,3,2,1:T(8,128)(2,1)}, bf16[512,1,5,128]{0,3,2,1:T(8,128)(2,1)S(1)}, u32[]{:S(2)}) copy-start(bf16[512,1,5,128]{0,3,2,1:T(8,128)(2,1)S(1)} %fusion.58) | copy-start | bytes 1966084
  104.3 2.7 copy-start.16
  134.8 0.9 copy-start.20
  134.8 148.9 %all-gather.2.cloned.1.call-start = ((), (), s32[]{:S(2)}) async-start(), calls=%async_computation.3 | async-start | bytes 6963200 | tf_op jit(solution)/shard_map/all_gather | solution.py:143
  136.2 25.1 %copy-start.9 = (f32[512,512]{1,0:T(8,128)}, f32[512,512]{1,0:T(8,128)S(1)}, u32[]{:S(2)}) copy-start(f32[512,512]{1,0:T(8,128)S(1)} %fusion.31) | copy-start | bytes 3145732
  142.0 8.7 %slice-start = ((s8[6553600]{0:T(1024)(128)(4,1)}), s8[4194304]{0:T(1024)(128)(4,1)S(1)}, s32[]{:S(2)}) async-start(s8[6553600]{0:T(1024)(128)(4,1)} %bitcast.527), calls=%async_computation.5 | async-start | bytes 8388608
  142.6 19.8 %copy-start.4 = (f32[512,1024]{1,0:T(8,128)}, f32[512,1024]{1,0:T(8,128)S(1)}, u32[]{:S(2)}) copy-start(f32[512,1024]{1,0:T(8,128)S(1)} %subtract_exponential_fusion.4) | copy-start | bytes 6291460
  144.6 6.1 %slice-start.1 = ((s8[6553600]{0:T(1024)(128)(4,1)}), s8[2359296]{0:T(1024)(128)(4,1)S(1)}, s32[]{:S(2)}) async-start(s8[6553600]{0:T(1024)(128)(4,1)} %bitcast.527), calls=%async_computation.6 | async-start | bytes 4718592
  150.7 10.1 %copy-start.19 = (bf16[512,1,5,128]{0,3,2,1:T(8,128)(2,1)S(1)}, bf16[512,1,5,128]{0,3,2,1:T(8,128)(2,1)}, u32[]{:S(2)}) copy-start(bf16[512,1,5,128]{0,3,2,1:T(8,128)(2,1)} %copy-done.18) | copy-start | bytes 1966084
  150.7 10.4 %copy-start.17 = (bf16[512,1,5,128]{0,3,2,1:T(8,128)(2,1)S(1)}, bf16[512,1,5,128]{0,3,2,1:T(8,128)(2,1)}, u32[]{:S(2)}) copy-start(bf16[512,1,5,128]{0,3,2,1:T(8,128)(2,1)} %copy-done.16) | copy-start | bytes 1966084
  218.5 1.9 copy-start.8
  218.5 2.2 copy-start.15
  220.3 1.2 copy-start.14
  220.7 1.7 copy-start.3
  222.3 1.2 copy-start.13
  222.8 1.7 copy-start.2
  224.5 1.2 copy-start.12
  225.0 1.7 copy-start.1
  226.7 1.2 copy-start.11
  227.2 1.7 copy-start
  228.9 1.2 copy-start.10
  233.4 1.6 copy-start.5
Sparse Core Ops, SparseCore 0:
  135.0 83.4 reduce-scatter.3
  220.9 62.8 all-gather.1

commit v4 on v0

--- a/solution.py
+++ b/solution.py
@@ -109,7 +109,7 @@
     weight_acc = contract_rows(flat_out, shard_rows)
     local_grad = contract_cols(shard_rows, out_weight).astype(jnp.bfloat16)
     weight_acc, output_gradient = (weight_acc, local_grad)
-    weight_total = lax.psum(weight_acc, "leaf").astype(jnp.bfloat16)
+    weight_total = lax.psum(weight_acc.astype(jnp.bfloat16), "leaf")
     key_acc = jnp.zeros((tree_len, kv_local, HEAD_SIZE), jnp.float32)
     value_acc = jnp.zeros((tree_len, kv_local, HEAD_SIZE), jnp.float32)
     query_parts = []

time: 454 us -> 268 us (0.59)
  blocking collectives: 289 us -> 27.6 us
  waiting for transfers between devices: 29.2 us -> 99.7 us
  local copies, waits for them, and re-layouts: 27.2 us -> 37 us
  starting transfers between devices: 11.2 us -> 5.97 us
    psum x1 -> x0, blocking collectives: 289 us -> none  [local(): weight_total = lax.psum(weight_acc, 'leaf').astype(jnp.bfloat16)]
    psum x0 -> x1, waiting for transfers between devices: none -> 70.5 us  [local(): weight_total = lax.psum(weight_acc.astype(jnp.bfloat16), 'leaf')]
    all_to_all x0 -> x1, blocking collectives: none -> 27.6 us  [local(): lax.all_to_all(gradients, 'ctx', split_axis=0, concat_axis=1, tiled=True)]
    unnamed x38 -> x85, local copies, waits for them, and re-layouts: 13 us -> 23.9 us
    all_to_all x1 -> x0, starting transfers between devices: 5.26 us -> none  [local(): lax.all_to_all(gradients, 'ctx', split_axis=0, concat_axis=1, tiled=True)]
  transfers between devices with their start and end apart: 3 -> 3, of which waited for: 1 -> 2; matrix products, arithmetic and copies ran while one was open for 11% -> 26% of each run, Pallas kernels for 0% -> 0%
where the time goes in v4:
time: 268 us; the launch traced here: 263 us
  waiting for transfers between devices  99.7 us (37%)
  matrix products  68.2 us (25%)
  local copies, waits for them, and re-layouts  37 us (14%)
  blocking collectives  27.6 us (10%)
  between operations  15.1 us (6%)
  other arithmetic  9.29 us (3%)
  starting transfers between devices  5.97 us (2%)
    psum x1, waiting for transfers between devices, local(): weight_total = lax.psum(weight_acc.astype(jnp.bfloat16), 'leaf')  70.5 us
    dot_general x21, matrix products, contract_cols(): lax.dot_general(left, right, (((1,), (1,)), ((), ())), preferred_element_...  35.1 us
    all_to_all x1, waiting for transfers between devices, local(): lax.all_to_all(query_key_value_rows, 'ctx', split_axis=1, concat_axis=0,...  28.5 us
    all_to_all x1, blocking collectives, local(): lax.all_to_all(gradients, 'ctx', split_axis=0, concat_axis=1, tiled=True)  27.6 us
    unnamed x85, local copies, waits for them, and re-layouts  23.9 us
    dot_general x21, matrix products, contract_rows(): lax.dot_general(left, right, (((0,), (0,)), ((), ())), preferred_element_...  18.5 us
    dot_general x10, matrix products, local(): jnp.dot(logit_cotangent, keys_now, preferred_element_type=jnp.float32)  6.97 us
    all_to_all x1, starting transfers between devices, local(): lax.all_to_all(query_key_value_rows, 'ctx', split_axis=1, concat_axis=0,...  5.93 us
  transfers between devices with their start and end apart: 3, of which 2 were waited for; matrix products, arithmetic and copies ran while one was open for 26% of the time, Pallas kernels for 0%

profile of v4, /device:TPU:1, one launch (start us, length us, event | category | flops | bytes accessed | tf_op | source)
XLA Modules:
  0.0 262.9 jit_solution(10882984462684887697)
XLA Ops:
  7.2 0.7 all-gather.2.cloned.1.call-update
  7.9 3.9 %copy.35 = bf16[128,7168]{0,1:T(8,128)(2,1)} copy(bf16[128,7168]{1,0:T(8,128)(2,1)} %param.47) | data formatting | bytes 3670016 | tf_op args[0]
  11.8 5.9 %all-to-all-start = ((bf16[128,8,896]{0,2,1:T(8,128)(2,1)}), bf16[128,8,896]{0,2,1:T(8,128)(2,1)S(1)}, u32[]{:S(2)}, u32[]{:S(2)}) async-start(bf16[128,8,896]{0,2,1:T(8,128)(2,1)} %bitcast.482), calls=%async_computation | async-start | bytes 3670016 | tf_op jit(solution)/shard_map/all_to_all | solution.py:60
  17.7 2.2 while.34
  20.0 1.6 broadcast_in_dim.71
  22.4 1.6 broadcast_in_dim.76
  24.0 0.8 fusion.14
  24.9 1.0 copy.42
  25.9 28.5 %all-to-all-done = bf16[128,8,896]{0,2,1:T(8,128)(2,1)S(1)} async-done(((bf16[128,8,896]{0,2,1:T(8,128)(2,1)}), bf16[128,8,896]{0,2,1:T(8,128)(2,1)S(1)}, u32[]{:S(2)}, u32[]{:S(2)}) %all-to-all-start) | async-done | bytes 1835040 | tf_op jit(solution)/shard_map/all_to_all | solution.py:60
  54.4 2.4 copy.36
  56.8 3.2 %reshape.966 = bf16[1024,1,7,128]{0,3,2,1:T(8,128)(2,1)S(1)} reshape(bf16[8,128,896]{1,0,2:T(8,128)(2,1)} %copy.36) | data formatting | bytes 3670016 | tf_op jit(solution)/shard_map/reshape | solution.py:64
  60.1 1.0 fusion.8
  61.1 1.1 exponential_reduce_fusion.1
  62.2 1.8 fusion.3
  64.1 2.2 exponential_reduce_fusion
  66.3 1.6 fusion.54
  67.9 3.2 %fusion.51 = bf16[512,1,5,128]{0,3,2,1:T(8,128)(2,1)S(1)} fusion(f32[1024,512,5]{1,0,2:T(8,128)S(1)} %get-tuple-element.332, f32[5,512]{1,0:T(8,128)S(1)} %log_add_fusion, f32[512]{0:T(512)S(1)} %get-tuple-element.330, pred[512,1024]{0,1:T(8,128)(4,1)S(1)} %copy.42, bf16[1024,1,7,128]{0,3,2,1:T(8,128)(2,1)S(1)} %reshape.966), kind=kOutput, calls=%fused_computation.80 | convolution fusion | flops 681902080 | bytes 11945984 | tf_op jit(solution)/shard_map/gjts,sgd->tgjd/dot_general | solution.py:97
  71.2 1.3 pad_maximum_fusion.1
  72.4 1.4 fusion.37
  73.9 1.4 fusion.33
  75.3 1.5 fusion.35
  76.8 1.4 fusion.31
  78.2 1.5 fusion.39
  79.6 2.0 subtract_exponential_fusion.1
  81.7 2.0 subtract_exponential_fusion.3
  83.7 2.0 subtract_exponential_fusion.2
  85.7 2.0 subtract_exponential_fusion.4
  87.7 2.0 subtract_exponential_fusion
  89.7 12.0 %convolution_convert_fusion.1 = bf16[1024,640]{0,1:T(8,128)(2,1)S(1)} fusion(bf16[1024,5120]{1,0:T(8,128)(2,1)} %all-gather.2.cloned.1.call-done, bf16[640,5120]{1,0:T(8,128)(2,1)} %param.49), kind=kOutput, calls=%fused_computation.36 | convolution fusion | flops 6711541760 | bytes 18350080 | tf_op jit(solution)/shard_map/dot_general | solution.py:53
  102.0 0.8 fusion.116
  102.7 0.6 copy-done.4
  103.3 0.5 multiply_convert_fusion.4
  103.8 1.1 convolution_convert_fusion.11
  104.9 1.3 fusion.149
  107.3 1.0 convolution_convert_fusion.5
  108.6 0.9 convolution_convert_fusion.4
  110.2 1.0 convolution_convert_fusion.6
  111.5 0.8 copy-done.8
  112.3 0.9 convolution_convert_fusion.2
  113.3 9.2 %convolution_convert_fusion = bf16[640,5120]{1,0:T(8,128)(2,1)} fusion(bf16[1024,640]{0,1:T(8,128)(2,1)S(1)} %bitcast.489, bf16[1024,5120]{1,0:T(8,128)(2,1)S(1)} %copy-done.38), kind=kOutput, calls=%fused_computation.10 | convolution fusion | flops 6714163200 | bytes 18350080 | tf_op jit(solution)/shard_map/dot_general | solution.py:47
  122.5 2.2 multiply_convert_fusion.1
  125.2 0.5 multiply_convert_fusion.3
  126.1 0.6 copy-done.2
  126.8 0.5 multiply_convert_fusion.2
  127.8 1.1 copy-done.1
  131.8 0.5 fusion.57
  132.7 0.5 fusion.58
  133.8 0.5 fusion.59
  135.0 0.5 fusion.70
  135.5 0.8 copy-done.5
  136.8 0.7 copy-done.24
  137.9 0.5 fusion.62
  138.4 0.7 copy-done.22
  139.5 0.5 fusion.63
  140.0 0.8 copy-done.18
  141.5 0.5 fusion.64
  142.0 0.8 copy-done.20
  143.1 0.5 fusion.71
  143.9 2.5 copy.45
  146.4 2.1 copy.56
  148.8 27.6 %all_to_all.35 = bf16[8,128,896]{1,2,0:T(8,128)(2,1)S(1)} all-to-all(bf16[8,128,896]{1,2,0:T(8,128)(2,1)S(1)} %copy.46), channel_id=1, replica_groups=mesh['leaf'=16,'ctx'=8] {'ctx'}, dimensions={0} | all-to-all | bytes 3670016 | tf_op jit(solution)/shard_map/all_to_all | solution.py:170
  176.3 2.9 %copy.47 = bf16[128,7168]{1,0:T(8,128)(2,1)} copy(bf16[128,7168]{0,1:T(8,128)(2,1)S(1)} %bitcast.485) | data formatting | bytes 3670016
  179.2 70.5 %all-reduce.3.cloned.1.call-done = bf16[640,5120]{1,0:T(8,128)(2,1)} async-done(((bf16[640,5120]{1,0:T(8,128)(2,1)}), bf16[640,5120]{1,0:T(8,128)(2,1)}) %all-reduce.3.cloned.1.call-update) | async-done | bytes 6553616 | tf_op jit(solution)/shard_map/psum | solution.py:112
  249.7 6.1 %copy.98 = bf16[640,5120]{1,0:T(8,128)(2,1)} copy(bf16[640,5120]{1,0:T(8,128)(2,1)} %all-reduce.3.cloned.1.call-done) | data formatting | bytes 13107200
  (147 shorter events, 14.4 us)
Async XLA Ops:
  7.2 82.6 %all-gather.2.cloned.1.call-start = ((), (), s32[]{:S(2)}) async-start(), calls=%async_computation.2 | async-start | bytes 11796480 | tf_op jit(solution)/shard_map/all_gather | solution.py:108
  11.8 6.0 %copy-start.39 = (s32[1,8]{1,0:T(1,128)S(1)}, s32[1,8]{1,0:T(1,128)}, u32[]{:S(2)}) copy-start(s32[1,8]{1,0:T(1,128)} %param.50) | copy-start | bytes 100
  11.8 42.6 %all-to-all-start = ((bf16[128,8,896]{0,2,1:T(8,128)(2,1)}), bf16[128,8,896]{0,2,1:T(8,128)(2,1)S(1)}, u32[]{:S(2)}, u32[]{:S(2)}) async-start(bf16[128,8,896]{0,2,1:T(8,128)(2,1)} %bitcast.482), calls=%async_computation | async-start | bytes 3670016 | tf_op jit(solution)/shard_map/all_to_all | solution.py:60
  17.7 232.0 %all-reduce.3.cloned.1.call-start = ((), (), s32[]{:S(2)}) async-start(), calls=%async_computation.3 | async-start | bytes 13107200 | tf_op jit(solution)/shard_map/psum | solution.py:112
  21.6 4.3 %copy-start.37 = (s32[1024]{0:T(1024)S(1)}, s32[1024]{0:T(1024)}, u32[]{:S(2)}) copy-start(s32[1024]{0:T(1024)} %param.51) | copy-start | bytes 12292
  67.9 3.3 %copy-start.28 = (bf16[512,1,5,128]{0,3,2,1:T(8,128)(2,1)}, bf16[512,1,5,128]{0,3,2,1:T(8,128)(2,1)S(1)}, u32[]{:S(2)}) copy-start(bf16[512,1,5,128]{0,3,2,1:T(8,128)(2,1)S(1)} %fusion.54) | copy-start | bytes 1966084
  71.1 2.7 %copy-start.26 = (bf16[512,1,5,128]{0,3,2,1:T(8,128)(2,1)}, bf16[512,1,5,128]{0,3,2,1:T(8,128)(2,1)S(1)}, u32[]{:S(2)}) copy-start(bf16[512,1,5,128]{0,3,2,1:T(8,128)(2,1)S(1)} %fusion.51) | copy-start | bytes 1966084
  89.7 12.0 %copy-start.29 = (bf16[512,1,5,128]{0,3,2,1:T(8,128)(2,1)S(1)}, bf16[512,1,5,128]{0,3,2,1:T(8,128)(2,1)}, u32[]{:S(2)}) copy-start(bf16[512,1,5,128]{0,3,2,1:T(8,128)(2,1)} %copy-done.28) | copy-start | bytes 1966084
  89.7 12.2 %copy-start.27 = (bf16[512,1,5,128]{0,3,2,1:T(8,128)(2,1)S(1)}, bf16[512,1,5,128]{0,3,2,1:T(8,128)(2,1)}, u32[]{:S(2)}) copy-start(bf16[512,1,5,128]{0,3,2,1:T(8,128)(2,1)} %copy-done.26) | copy-start | bytes 1966084
  89.7 23.6 %copy-start.38 = (bf16[1024,5120]{1,0:T(8,128)(2,1)S(1)}, bf16[1024,5120]{1,0:T(8,128)(2,1)}, u32[]{:S(2)}) copy-start(bf16[1024,5120]{1,0:T(8,128)(2,1)} %all-gather.2.cloned.1.call-done) | copy-start | bytes 31457284
  101.7 1.6 copy-start.4
  103.8 2.4 copy-start.17
  104.9 2.0 copy-start.23
  106.6 2.0 copy-start.6
  106.6 1.6 copy-start.21
  107.2 1.0 copy-start.12
  107.2 2.3 copy-start.16
  108.6 1.6 copy-start.10
  109.5 1.7 copy-start.19
  110.2 1.0 copy-start.14
  110.2 3.1 %copy-start.30 = (bf16[1024,1,5,128]{0,3,2,1:T(8,128)(2,1)S(1)}, bf16[1024,1,5,128]{0,3,2,1:T(8,128)(2,1)}, u32[]{:S(2)}) copy-start(bf16[1024,1,5,128]{0,3,2,1:T(8,128)(2,1)} %pad_maximum_fusion.1) | copy-start | bytes 3932164
  111.5 0.8 copy-start.8
  122.5 2.7 %copy-start.3 = (f32[512,1024]{1,0:T(8,128)S(1)}, f32[512,1024]{1,0:T(8,128)}, u32[]{:S(2)}) copy-start(f32[512,1024]{1,0:T(8,128)} %subtract_exponential_fusion.3) | copy-start | bytes 6291460
  122.5 2.7 %copy-start.36 = (f32[512]{0:T(512)S(1)}, f32[512]{0:T(512)}, u32[]{:S(2)}) copy-start(f32[512]{0:T(512)} %get-tuple-element.304) | copy-start | bytes 6148
  125.2 1.6 copy-start.2
  126.8 1.0 copy-start.25
  127.3 1.6 copy-start.1
  128.9 1.0 copy-start.34
  128.9 1.0 copy-start.35
  129.4 0.9 copy-start.32
  129.4 1.0 copy-start.31
  129.4 1.1 copy-start.33
  129.4 1.2 copy-start.15
  130.3 1.1 copy-start.13
  131.0 1.3 copy-start.11
  132.3 1.1 copy-start.7
  133.4 1.2 copy-start.9
  134.6 1.6 copy-start.5
  136.3 1.2 copy-start.24
  137.9 1.2 copy-start.22
  139.5 1.3 copy-start.18
  139.5 2.0 copy-start
  141.5 1.3 copy-start.20
Sparse Core Ops, SparseCore 0:
  9.7 75.9 all-gather.1
  122.6 127.0 all-reduce.2
